TPU v7x, 128 devices: a whole 4x4x4 slice. The times are simulated.
128 devices in a mesh: loop: 64 (over x, z, y), grp: 2 (over core).
Axes of the slice: x: 4, y: 4, z: 4, core: 2. Of those that a mesh axis runs over, the one named last changes fastest.
Arguments:
- particles: bfloat16 [8192, 3456], P('loop'), may hold values from -32 to 32
- references: bfloat16 [256, 3456], P(('loop', 'grp')), may hold values from -6 to 6
- classes: int32 [8192], P(('loop', 'grp')), may hold values from 0 to 255, as said below
- angles: int32 [8192], P(('loop', 'grp')), may hold values from 0 to 71
- weights: int32 [8192], P(('loop', 'grp')), may hold values from 1 to 4
Outputs:
- log_evidence: float32 [8192], P(('loop', 'grp'))
- class_average: float32 [256, 3456], P(('loop', 'grp'))
Inputs may be any that keep to these rules, and one draw needn't show every extreme that they name: Call the classes c with the same value of c // 4 the classes of one owner. In each aligned block of 64 rows at most 2 particles name the classes of one owner, and one owner receives exactly 2 from every block. Every class is named by some particle.
All inputs are finite; a program needn't handle non-finite values.
Results may differ from a plain program's by a relative error of at most 0.0003.
Values may be sent and summed in bfloat16 or wider, within the bound.
No kernel may reach another device: no remote copies, remote signals or barrier semaphores. Data moves between devices by JAX's collectives and lax.ppermute only.
A program may use at most 128 MiB of HBM per device.

v0:
```python
import math
import jax
import jax.numpy as jnp
from jax import lax
from jax.sharding import PartitionSpec as P

RADII = 48
ANGLES = 72
score_factor = 2.0


def turned_rows(ref_block, radius_count, angle_count):
    block_rows = ref_block.shape[0]
    polar_rows = ref_block.reshape(block_rows, radius_count, angle_count)
    angle_grid = jnp.arange(angle_count, dtype=jnp.int32)
    source_index = (angle_grid[:, None] + angle_grid[None, :]) % angle_count
    rotated = jnp.take(polar_rows, source_index, axis=2)
    rotated = jnp.transpose(rotated, (0, 2, 1, 3))
    return rotated.reshape(block_rows * angle_count, radius_count * angle_count)


def group_of():
    for group_size in (16, 8, 4, 2):
        return group_size
    return 1


def empty_stats(row_count):
    return (jnp.full((row_count,), -jnp.inf, jnp.float32), jnp.zeros((row_count,), jnp.float32))


def score_all(images, gathered):
    flat_len = images.shape[1]
    score_scale = score_factor / math.sqrt(flat_len)
    ref_count = gathered.shape[0]
    group_size = group_of()
    ref_groups = gathered.reshape(ref_count // group_size, group_size, flat_len)

    def advance(current, ref_block):
        highest, summed = current
        rotated = turned_rows(ref_block, RADII, ANGLES)
        scores = (
            lax.dot_general(
                images, rotated, (((1,), (1,)), ((), ())), preferred_element_type=jnp.float32
            )
            * score_scale
        )
        new_max = jnp.maximum(highest, jnp.max(scores, axis=1))
        summed = summed * jnp.exp(highest - new_max) + jnp.sum(
            jnp.exp(scores - new_max[:, None]), axis=1
        )
        return ((new_max, summed), None)

    result, _ = lax.scan(advance, empty_stats(images.shape[0]), ref_groups)
    return result


def local(particles, references, classes, angles, weights):
    row_count, flat_len = particles.shape
    grp_size = lax.axis_size("grp")
    half_rows = row_count // grp_size
    grp_index = lax.axis_index("grp")
    own_rows = lax.dynamic_slice_in_dim(particles, grp_index * half_rows, half_rows, 0)
    gathered = lax.all_gather(references, "loop", axis=0, tiled=True)
    highest, summed = score_all(particles, gathered)
    joint_max = lax.pmax(highest, "grp")
    summed = lax.psum(summed * jnp.exp(highest - joint_max), "grp")
    highest = joint_max
    highest = lax.dynamic_slice_in_dim(highest, grp_index * half_rows, half_rows, 0)
    summed = lax.dynamic_slice_in_dim(summed, grp_index * half_rows, half_rows, 0)
    log_evidence = highest + jnp.log(summed)
    owner_count = lax.axis_size("loop")
    per_owner = references.shape[0] * grp_size
    capacity = max(2, row_count // owner_count)
    slot_count = owner_count * capacity
    owner_of = classes // per_owner
    member_of = classes % per_owner
    owner_hits = (owner_of[:, None] == jnp.arange(owner_count, dtype=jnp.int32)[None, :]).astype(
        jnp.int32
    )
    earlier = jnp.cumsum(owner_hits, axis=0) - owner_hits
    slot_index = jnp.sum(earlier * owner_hits, axis=1)
    target_slot = owner_of * capacity + slot_index
    placement = (jnp.arange(slot_count, dtype=jnp.int32)[:, None] == target_slot[None, :]).astype(
        jnp.bfloat16
    )
    outgoing = jnp.dot(placement, own_rows, preferred_element_type=jnp.float32).astype(jnp.bfloat16)
    outgoing = outgoing.reshape(owner_count, capacity, flat_len)
    labels = jnp.stack([member_of, angles, weights], axis=1).astype(jnp.bfloat16)
    labels_out = jnp.dot(placement, labels, preferred_element_type=jnp.float32).astype(jnp.bfloat16)
    labels_out = labels_out.reshape(owner_count, capacity, 3)
    incoming, labels_in = (
        lax.all_to_all(outgoing, "loop", split_axis=0, concat_axis=0, tiled=True),
        lax.all_to_all(labels_out, "loop", split_axis=0, concat_axis=0, tiled=True),
    )
    images = incoming.reshape(slot_count, RADII, ANGLES)
    labels_in = labels_in.reshape(slot_count, 3).astype(jnp.float32)
    member_in = labels_in[:, 0]
    rotation = labels_in[:, 1]
    weight_of = labels_in[:, 2]
    angle_grid = jnp.arange(ANGLES, dtype=jnp.float32)
    source_angle = jnp.mod(angle_grid[None, :] - rotation[:, None], float(ANGLES))
    rotator = (angle_grid[None, :, None] == source_angle[:, None, :]).astype(jnp.bfloat16)
    aligned = jnp.einsum("srt,stf->srf", images, rotator, preferred_element_type=jnp.float32)
    aligned = aligned.astype(jnp.bfloat16).reshape(slot_count, flat_len)
    member_grid = jnp.arange(per_owner, dtype=jnp.float32)
    weighted = (
        (member_grid[:, None] == member_in[None, :]).astype(jnp.float32) * weight_of[None, :]
    ).astype(jnp.bfloat16)
    partial_sums = jnp.dot(weighted, aligned, preferred_element_type=jnp.float32)
    partial_weight = jnp.sum(weighted.astype(jnp.float32), axis=1)
    class_sums, class_weight = (
        lax.psum_scatter(partial_sums, "grp", scatter_dimension=0, tiled=True),
        lax.psum_scatter(partial_weight, "grp", scatter_dimension=0, tiled=True),
    )
    class_average = class_sums / class_weight[:, None]
    return (log_evidence, class_average)


def solution(mesh):
    return jax.shard_map(
        local,
        mesh=mesh,
        in_specs=(
            P("loop", None),
            P(("loop", "grp"), None),
            P(("loop", "grp")),
            P(("loop", "grp")),
            P(("loop", "grp")),
        ),
        out_specs=(P(("loop", "grp")), P(("loop", "grp"), None)),
        check_vma=False,
    )
```

profile of v0, /device:TPU:1, one launch (start us, length us, event | category | flops | bytes accessed | tf_op | source)
XLA Modules:
  0.0 887.3 jit_solution(3810419134806905992)
XLA Ops:
  3.2 12.2 %all-to-all-start = ((bf16[64,2,3]{2,1,0:T(2,128)(2,1)}), bf16[64,2,3]{2,1,0:T(2,128)(2,1)}, u32[]{:S(2)}, u32[]{:S(2)}) async-start(bf16[64,2,3]{2,1,0:T(2,128)(2,1)} %bitcast.4), calls=%async_computation | async-start | bytes 65536 | tf_op jit(solution)/shard_map/all_to_all | solution.py:94
  15.5 153.3 %all-gather = bf16[64,2,3456]{2,1,0:T(2,128)(2,1)S(1)} all-gather(bf16[1,2,3456]{2,1,0:T(2,128)(2,1)} %bitcast.39), channel_id=1, replica_groups=mesh['loop'=64,'grp'=2] {'loop'}, dimensions={0}, use_global_device_ids=true | all-gather | bytes 898560 | tf_op jit(solution)/shard_map/all_gather | solution.py:64
  169.2 649.2 %while.15 = (s32[]{:T(128)}, f32[128]{0:T(128)S(1)}, f32[128]{0:T(128)S(1)}, bf16[8,16,3456]{2,1,0:T(8,128)(2,1)S(1)}, bf16[128,3456]{1,0:T(8,128)(2,1)}, /*index=5*/s32[]{:T(128)}, s32[]{:T(128)}) while((s32[]{:T(128)}, f32[128]{0:T(128)S(1)}, f32[128]{0:T(128)S(1)}, bf16[8,16,3456]{2,1,0:T(8,128)(2,1)S(1)}, ...), condition=%wide.region_3.4_spmd.clone, body=%wide.region_0.3_spmd.clone.sunk | while | flops 1023913024 | bytes 78075904 | solution.py:54
  170.0 16.7 %gather_fusion = bf16[5184,16,48]{2,1,0:T(8,128)(2,1)} fusion(bf16[16,48,72]{1,0,2:T(8,128)(2,1)S(1)} %copy.31, s32[6144]{0:T(1024)S(1)} %pad_clamp_fusion.2), kind=kCustom, calls=%fused_computation.clone.clone.1 | custom fusion | bytes 15945984 | tf_op jit(solution)/shard_map/while/body/eval_jaxpr/jit(_take)/gather | solution.py:17
  186.8 24.6 %copy.32 = bf16[72,72,16,48]{1,3,0,2:T(8,128)(2,1)} copy(bf16[72,72,16,48]{3,2,1,0:T(8,128)(2,1)} %bitcast.37) | data formatting | bytes 15925248 | tf_op jit(solution)/shard_map/while/body/eval_jaxpr/jit(_take)/gather | solution.py:17
  211.4 10.6 %select_bitcast_fusion.2 = bf16[16,72,48,72]{3,2,1,0:T(8,128)(2,1)} fusion(bf16[72,72,16,48]{1,3,0,2:T(8,128)(2,1)} %copy.32, pred[72,72]{1,0:T(8,128)(4,1)S(1)} %compare_and_fusion.2), kind=kLoop, calls=%fused_computation.1.clone.1 | loop fusion | flops 3981312 | bytes 15930432 | tf_op jit(solution)/shard_map/while/body/eval_jaxpr/jit(_take)/select_n | solution.py:17
  222.1 22.6 %reshape.157 = bf16[1152,3456]{1,0:T(8,128)(2,1)} reshape(bf16[16,72,48,72]{3,2,1,0:T(8,128)(2,1)} %select_bitcast_fusion.2) | data formatting | bytes 15925248 | tf_op jit(solution)/shard_map/while/body/eval_jaxpr/reshape | solution.py:19
  244.6 5.5 fusion.45
  251.2 16.7 %gather_fusion = bf16[5184,16,48]{2,1,0:T(8,128)(2,1)} fusion(bf16[16,48,72]{1,0,2:T(8,128)(2,1)S(1)} %copy.31, s32[6144]{0:T(1024)S(1)} %pad_clamp_fusion.2), kind=kCustom, calls=%fused_computation.clone.clone.1 | custom fusion | bytes 15945984 | tf_op jit(solution)/shard_map/while/body/eval_jaxpr/jit(_take)/gather | solution.py:17
  267.9 24.6 %copy.32 = bf16[72,72,16,48]{1,3,0,2:T(8,128)(2,1)} copy(bf16[72,72,16,48]{3,2,1,0:T(8,128)(2,1)} %bitcast.37) | data formatting | bytes 15925248 | tf_op jit(solution)/shard_map/while/body/eval_jaxpr/jit(_take)/gather | solution.py:17
  292.6 10.6 %select_bitcast_fusion.2 = bf16[16,72,48,72]{3,2,1,0:T(8,128)(2,1)} fusion(bf16[72,72,16,48]{1,3,0,2:T(8,128)(2,1)} %copy.32, pred[72,72]{1,0:T(8,128)(4,1)S(1)} %compare_and_fusion.2), kind=kLoop, calls=%fused_computation.1.clone.1 | loop fusion | flops 3981312 | bytes 15930432 | tf_op jit(solution)/shard_map/while/body/eval_jaxpr/jit(_take)/select_n | solution.py:17
  303.2 22.6 %reshape.157 = bf16[1152,3456]{1,0:T(8,128)(2,1)} reshape(bf16[16,72,48,72]{3,2,1,0:T(8,128)(2,1)} %select_bitcast_fusion.2) | data formatting | bytes 15925248 | tf_op jit(solution)/shard_map/while/body/eval_jaxpr/reshape | solution.py:19
  325.8 5.5 fusion.45
  332.3 16.7 %gather_fusion = bf16[5184,16,48]{2,1,0:T(8,128)(2,1)} fusion(bf16[16,48,72]{1,0,2:T(8,128)(2,1)S(1)} %copy.31, s32[6144]{0:T(1024)S(1)} %pad_clamp_fusion.2), kind=kCustom, calls=%fused_computation.clone.clone.1 | custom fusion | bytes 15945984 | tf_op jit(solution)/shard_map/while/body/eval_jaxpr/jit(_take)/gather | solution.py:17
  349.1 24.6 %copy.32 = bf16[72,72,16,48]{1,3,0,2:T(8,128)(2,1)} copy(bf16[72,72,16,48]{3,2,1,0:T(8,128)(2,1)} %bitcast.37) | data formatting | bytes 15925248 | tf_op jit(solution)/shard_map/while/body/eval_jaxpr/jit(_take)/gather | solution.py:17
  373.7 10.6 %select_bitcast_fusion.2 = bf16[16,72,48,72]{3,2,1,0:T(8,128)(2,1)} fusion(bf16[72,72,16,48]{1,3,0,2:T(8,128)(2,1)} %copy.32, pred[72,72]{1,0:T(8,128)(4,1)S(1)} %compare_and_fusion.2), kind=kLoop, calls=%fused_computation.1.clone.1 | loop fusion | flops 3981312 | bytes 15930432 | tf_op jit(solution)/shard_map/while/body/eval_jaxpr/jit(_take)/select_n | solution.py:17
  384.4 22.6 %reshape.157 = bf16[1152,3456]{1,0:T(8,128)(2,1)} reshape(bf16[16,72,48,72]{3,2,1,0:T(8,128)(2,1)} %select_bitcast_fusion.2) | data formatting | bytes 15925248 | tf_op jit(solution)/shard_map/while/body/eval_jaxpr/reshape | solution.py:19
  407.0 5.5 fusion.45
  413.5 16.7 %gather_fusion = bf16[5184,16,48]{2,1,0:T(8,128)(2,1)} fusion(bf16[16,48,72]{1,0,2:T(8,128)(2,1)S(1)} %copy.31, s32[6144]{0:T(1024)S(1)} %pad_clamp_fusion.2), kind=kCustom, calls=%fused_computation.clone.clone.1 | custom fusion | bytes 15945984 | tf_op jit(solution)/shard_map/while/body/eval_jaxpr/jit(_take)/gather | solution.py:17
  430.2 24.6 %copy.32 = bf16[72,72,16,48]{1,3,0,2:T(8,128)(2,1)} copy(bf16[72,72,16,48]{3,2,1,0:T(8,128)(2,1)} %bitcast.37) | data formatting | bytes 15925248 | tf_op jit(solution)/shard_map/while/body/eval_jaxpr/jit(_take)/gather | solution.py:17
  454.9 10.6 %select_bitcast_fusion.2 = bf16[16,72,48,72]{3,2,1,0:T(8,128)(2,1)} fusion(bf16[72,72,16,48]{1,3,0,2:T(8,128)(2,1)} %copy.32, pred[72,72]{1,0:T(8,128)(4,1)S(1)} %compare_and_fusion.2), kind=kLoop, calls=%fused_computation.1.clone.1 | loop fusion | flops 3981312 | bytes 15930432 | tf_op jit(solution)/shard_map/while/body/eval_jaxpr/jit(_take)/select_n | solution.py:17
  465.5 22.6 %reshape.157 = bf16[1152,3456]{1,0:T(8,128)(2,1)} reshape(bf16[16,72,48,72]{3,2,1,0:T(8,128)(2,1)} %select_bitcast_fusion.2) | data formatting | bytes 15925248 | tf_op jit(solution)/shard_map/while/body/eval_jaxpr/reshape | solution.py:19
  488.1 5.5 fusion.45
  494.6 16.7 %gather_fusion = bf16[5184,16,48]{2,1,0:T(8,128)(2,1)} fusion(bf16[16,48,72]{1,0,2:T(8,128)(2,1)S(1)} %copy.31, s32[6144]{0:T(1024)S(1)} %pad_clamp_fusion.2), kind=kCustom, calls=%fused_computation.clone.clone.1 | custom fusion | bytes 15945984 | tf_op jit(solution)/shard_map/while/body/eval_jaxpr/jit(_take)/gather | solution.py:17
  511.4 24.6 %copy.32 = bf16[72,72,16,48]{1,3,0,2:T(8,128)(2,1)} copy(bf16[72,72,16,48]{3,2,1,0:T(8,128)(2,1)} %bitcast.37) | data formatting | bytes 15925248 | tf_op jit(solution)/shard_map/while/body/eval_jaxpr/jit(_take)/gather | solution.py:17
  536.1 10.6 %select_bitcast_fusion.2 = bf16[16,72,48,72]{3,2,1,0:T(8,128)(2,1)} fusion(bf16[72,72,16,48]{1,3,0,2:T(8,128)(2,1)} %copy.32, pred[72,72]{1,0:T(8,128)(4,1)S(1)} %compare_and_fusion.2), kind=kLoop, calls=%fused_computation.1.clone.1 | loop fusion | flops 3981312 | bytes 15930432 | tf_op jit(solution)/shard_map/while/body/eval_jaxpr/jit(_take)/select_n | solution.py:17
  546.7 22.6 %reshape.157 = bf16[1152,3456]{1,0:T(8,128)(2,1)} reshape(bf16[16,72,48,72]{3,2,1,0:T(8,128)(2,1)} %select_bitcast_fusion.2) | data formatting | bytes 15925248 | tf_op jit(solution)/shard_map/while/body/eval_jaxpr/reshape | solution.py:19
  569.3 5.5 fusion.45
  575.8 16.7 %gather_fusion = bf16[5184,16,48]{2,1,0:T(8,128)(2,1)} fusion(bf16[16,48,72]{1,0,2:T(8,128)(2,1)S(1)} %copy.31, s32[6144]{0:T(1024)S(1)} %pad_clamp_fusion.2), kind=kCustom, calls=%fused_computation.clone.clone.1 | custom fusion | bytes 15945984 | tf_op jit(solution)/shard_map/while/body/eval_jaxpr/jit(_take)/gather | solution.py:17
  592.5 24.6 %copy.32 = bf16[72,72,16,48]{1,3,0,2:T(8,128)(2,1)} copy(bf16[72,72,16,48]{3,2,1,0:T(8,128)(2,1)} %bitcast.37) | data formatting | bytes 15925248 | tf_op jit(solution)/shard_map/while/body/eval_jaxpr/jit(_take)/gather | solution.py:17
  617.2 10.6 %select_bitcast_fusion.2 = bf16[16,72,48,72]{3,2,1,0:T(8,128)(2,1)} fusion(bf16[72,72,16,48]{1,3,0,2:T(8,128)(2,1)} %copy.32, pred[72,72]{1,0:T(8,128)(4,1)S(1)} %compare_and_fusion.2), kind=kLoop, calls=%fused_computation.1.clone.1 | loop fusion | flops 3981312 | bytes 15930432 | tf_op jit(solution)/shard_map/while/body/eval_jaxpr/jit(_take)/select_n | solution.py:17
  627.8 22.6 %reshape.157 = bf16[1152,3456]{1,0:T(8,128)(2,1)} reshape(bf16[16,72,48,72]{3,2,1,0:T(8,128)(2,1)} %select_bitcast_fusion.2) | data formatting | bytes 15925248 | tf_op jit(solution)/shard_map/while/body/eval_jaxpr/reshape | solution.py:19
  650.4 5.5 fusion.45
  656.9 16.7 %gather_fusion = bf16[5184,16,48]{2,1,0:T(8,128)(2,1)} fusion(bf16[16,48,72]{1,0,2:T(8,128)(2,1)S(1)} %copy.31, s32[6144]{0:T(1024)S(1)} %pad_clamp_fusion.2), kind=kCustom, calls=%fused_computation.clone.clone.1 | custom fusion | bytes 15945984 | tf_op jit(solution)/shard_map/while/body/eval_jaxpr/jit(_take)/gather | solution.py:17
  673.7 24.6 %copy.32 = bf16[72,72,16,48]{1,3,0,2:T(8,128)(2,1)} copy(bf16[72,72,16,48]{3,2,1,0:T(8,128)(2,1)} %bitcast.37) | data formatting | bytes 15925248 | tf_op jit(solution)/shard_map/while/body/eval_jaxpr/jit(_take)/gather | solution.py:17
  698.4 10.6 %select_bitcast_fusion.2 = bf16[16,72,48,72]{3,2,1,0:T(8,128)(2,1)} fusion(bf16[72,72,16,48]{1,3,0,2:T(8,128)(2,1)} %copy.32, pred[72,72]{1,0:T(8,128)(4,1)S(1)} %compare_and_fusion.2), kind=kLoop, calls=%fused_computation.1.clone.1 | loop fusion | flops 3981312 | bytes 15930432 | tf_op jit(solution)/shard_map/while/body/eval_jaxpr/jit(_take)/select_n | solution.py:17
  709.0 22.6 %reshape.157 = bf16[1152,3456]{1,0:T(8,128)(2,1)} reshape(bf16[16,72,48,72]{3,2,1,0:T(8,128)(2,1)} %select_bitcast_fusion.2) | data formatting | bytes 15925248 | tf_op jit(solution)/shard_map/while/body/eval_jaxpr/reshape | solution.py:19
  731.6 5.5 fusion.45
  738.1 16.7 %gather_fusion = bf16[5184,16,48]{2,1,0:T(8,128)(2,1)} fusion(bf16[16,48,72]{1,0,2:T(8,128)(2,1)S(1)} %copy.31, s32[6144]{0:T(1024)S(1)} %pad_clamp_fusion.2), kind=kCustom, calls=%fused_computation.clone.clone.1 | custom fusion | bytes 15945984 | tf_op jit(solution)/shard_map/while/body/eval_jaxpr/jit(_take)/gather | solution.py:17
  754.9 24.6 %copy.32 = bf16[72,72,16,48]{1,3,0,2:T(8,128)(2,1)} copy(bf16[72,72,16,48]{3,2,1,0:T(8,128)(2,1)} %bitcast.37) | data formatting | bytes 15925248 | tf_op jit(solution)/shard_map/while/body/eval_jaxpr/jit(_take)/gather | solution.py:17
  779.5 10.6 %select_bitcast_fusion.2 = bf16[16,72,48,72]{3,2,1,0:T(8,128)(2,1)} fusion(bf16[72,72,16,48]{1,3,0,2:T(8,128)(2,1)} %copy.32, pred[72,72]{1,0:T(8,128)(4,1)S(1)} %compare_and_fusion.2), kind=kLoop, calls=%fused_computation.1.clone.1 | loop fusion | flops 3981312 | bytes 15930432 | tf_op jit(solution)/shard_map/while/body/eval_jaxpr/jit(_take)/select_n | solution.py:17
  790.2 22.6 %reshape.157 = bf16[1152,3456]{1,0:T(8,128)(2,1)} reshape(bf16[16,72,48,72]{3,2,1,0:T(8,128)(2,1)} %select_bitcast_fusion.2) | data formatting | bytes 15925248 | tf_op jit(solution)/shard_map/while/body/eval_jaxpr/reshape | solution.py:19
  812.7 5.5 fusion.45
  821.1 31.1 %pmax.7 = f32[128]{0:T(128)S(1)} all-reduce(f32[128]{0:T(128)S(1)} %get-tuple-element.69), channel_id=1, replica_groups=mesh['loop'=64,'grp'=2] {'grp'}, use_global_device_ids=true, to_apply=%region_4.5 | all-reduce | flops 128 | bytes 1024 | tf_op jit(solution)/shard_map/pmax | solution.py:66
  852.2 4.6 all-to-all-start.1
  859.5 13.0 %all-to-all-done.1 = bf16[64,2,3456]{2,1,0:T(2,128)(2,1)S(1)} async-done(((bf16[64,2,3456]{2,1,0:T(2,128)(2,1)}), bf16[64,2,3456]{2,1,0:T(2,128)(2,1)S(1)}, u32[]{:S(2)}, u32[]{:S(2)}) %all-to-all-start.1) | async-done | bytes 884768 | tf_op jit(solution)/shard_map/all_to_all | solution.py:93
  872.5 3.4 reshape.125
  880.4 5.5 all-reduce.2
  (139 shorter events, 21.4 us)
Async XLA Ops:
  1.7 13.8 %copy-start.1 = (s32[64]{0:T(128)}, s32[64]{0:T(128)S(1)}, u32[]{:S(2)}) copy-start(s32[64]{0:T(128)S(1)} %multiply_add_fusion) | copy-start | bytes 772
  3.2 849.0 %all-to-all-start = ((bf16[64,2,3]{2,1,0:T(2,128)(2,1)}), bf16[64,2,3]{2,1,0:T(2,128)(2,1)}, u32[]{:S(2)}, u32[]{:S(2)}) async-start(bf16[64,2,3]{2,1,0:T(2,128)(2,1)} %bitcast.4), calls=%async_computation | async-start | bytes 65536 | tf_op jit(solution)/shard_map/all_to_all | solution.py:94
  169.2 649.3 %copy-start.2 = (s32[64]{0:T(128)S(1)}, s32[64]{0:T(128)}, u32[]{:S(2)}) copy-start(s32[64]{0:T(128)} %copy-done.1) | copy-start | bytes 772
  169.2 687.7 %copy-start.3 = (u32[128]{0:T(128)S(1)}, u32[128]{0:T(128)}, u32[]{:S(2)}) copy-start(u32[128]{0:T(128)} %constant.129) | copy-start | bytes 1540
  222.1 22.6 %copy-start = (bf16[128,3456]{1,0:T(8,128)(2,1)S(1)}, bf16[128,3456]{1,0:T(8,128)(2,1)}, u32[]{:S(2)}) copy-start(bf16[128,3456]{1,0:T(8,128)(2,1)} %get-tuple-element.163) | copy-start | bytes 2654212 | tf_op jit(solution)/shard_map/while
  303.2 22.6 %copy-start = (bf16[128,3456]{1,0:T(8,128)(2,1)S(1)}, bf16[128,3456]{1,0:T(8,128)(2,1)}, u32[]{:S(2)}) copy-start(bf16[128,3456]{1,0:T(8,128)(2,1)} %get-tuple-element.163) | copy-start | bytes 2654212 | tf_op jit(solution)/shard_map/while
  384.4 22.6 %copy-start = (bf16[128,3456]{1,0:T(8,128)(2,1)S(1)}, bf16[128,3456]{1,0:T(8,128)(2,1)}, u32[]{:S(2)}) copy-start(bf16[128,3456]{1,0:T(8,128)(2,1)} %get-tuple-element.163) | copy-start | bytes 2654212 | tf_op jit(solution)/shard_map/while
  465.5 22.6 %copy-start = (bf16[128,3456]{1,0:T(8,128)(2,1)S(1)}, bf16[128,3456]{1,0:T(8,128)(2,1)}, u32[]{:S(2)}) copy-start(bf16[128,3456]{1,0:T(8,128)(2,1)} %get-tuple-element.163) | copy-start | bytes 2654212 | tf_op jit(solution)/shard_map/while
  546.7 22.6 %copy-start = (bf16[128,3456]{1,0:T(8,128)(2,1)S(1)}, bf16[128,3456]{1,0:T(8,128)(2,1)}, u32[]{:S(2)}) copy-start(bf16[128,3456]{1,0:T(8,128)(2,1)} %get-tuple-element.163) | copy-start | bytes 2654212 | tf_op jit(solution)/shard_map/while
  627.8 22.6 %copy-start = (bf16[128,3456]{1,0:T(8,128)(2,1)S(1)}, bf16[128,3456]{1,0:T(8,128)(2,1)}, u32[]{:S(2)}) copy-start(bf16[128,3456]{1,0:T(8,128)(2,1)} %get-tuple-element.163) | copy-start | bytes 2654212 | tf_op jit(solution)/shard_map/while
  709.0 22.6 %copy-start = (bf16[128,3456]{1,0:T(8,128)(2,1)S(1)}, bf16[128,3456]{1,0:T(8,128)(2,1)}, u32[]{:S(2)}) copy-start(bf16[128,3456]{1,0:T(8,128)(2,1)} %get-tuple-element.163) | copy-start | bytes 2654212 | tf_op jit(solution)/shard_map/while
  790.2 22.6 %copy-start = (bf16[128,3456]{1,0:T(8,128)(2,1)S(1)}, bf16[128,3456]{1,0:T(8,128)(2,1)}, u32[]{:S(2)}) copy-start(bf16[128,3456]{1,0:T(8,128)(2,1)} %get-tuple-element.163) | copy-start | bytes 2654212 | tf_op jit(solution)/shard_map/while
  852.2 20.4 %all-to-all-start.1 = ((bf16[64,2,3456]{2,1,0:T(2,128)(2,1)}), bf16[64,2,3456]{2,1,0:T(2,128)(2,1)S(1)}, u32[]{:S(2)}, u32[]{:S(2)}) async-start(bf16[64,2,3456]{2,1,0:T(2,128)(2,1)} %reshape.124), calls=%async_computation.1 | async-start | bytes 1769472 | tf_op jit(solution)/shard_map/all_to_all | solution.py:93
where the time goes:
time: 897 us; the launch traced here: 887 us
  local copies, waits for them, and re-layouts  527 us (59%)
  blocking collectives  190 us (21%)
  other arithmetic  90.5 us (10%)
  matrix products  48 us (5%)
  starting transfers between devices  16.9 us (2%)
  waiting for transfers between devices  13 us (1%)
    gather x16, local copies, waits for them, and re-layouts, turned_rows(): rotated = jnp.take(polar_rows, source_index, axis=2)  331 us
    reshape x8, local copies, waits for them, and re-layouts, turned_rows(): return rotated.reshape(block_rows * angle_count, radius_count * angle_count)  181 us
    all_gather x1, blocking collectives, local(): gathered = lax.all_gather(references, 'loop', axis=0, tiled=True)  153 us
    select_n x16, other arithmetic, turned_rows(): rotated = jnp.take(polar_rows, source_index, axis=2)  85.3 us
    dot_general x8, matrix products, advance(): lax.dot_general(images, rotated, (((1,), (1,)), ((), ())), preferred_elem...  44 us
    pmax x1, blocking collectives, local(): joint_max = lax.pmax(highest, 'grp')  31.1 us
  transfers between devices with their start and end apart: 2, of which 1 were waited for; matrix products, arithmetic and copies ran while one was open for 74% of the time, Pallas kernels for 0%

commit v1 on v0

--- a/solution.py
+++ b/solution.py
@@ -61,7 +61,8 @@
     half_rows = row_count // grp_size
     grp_index = lax.axis_index("grp")
     own_rows = lax.dynamic_slice_in_dim(particles, grp_index * half_rows, half_rows, 0)
-    gathered = lax.all_gather(references, "loop", axis=0, tiled=True)
+    sent = jnp.stack([references] * lax.axis_size("loop"))
+    gathered = jnp.concatenate(lax.all_to_all(sent, "loop", 0, 0), axis=0)
     highest, summed = score_all(particles, gathered)
     joint_max = lax.pmax(highest, "grp")
     summed = lax.psum(summed * jnp.exp(highest - joint_max), "grp")

time: 897 us -> 727 us (0.81)
  blocking collectives: 190 us -> 9.39 us
    all_gather x1 -> x0, blocking collectives: 153 us -> none  [local(): gathered = lax.all_gather(references, 'loop', axis=0, tiled=True)]
    pmax x1, blocking collectives: 31.1 us -> 5.65 us  [local(): joint_max = lax.pmax(highest, 'grp')]
    all_to_all x1, waiting for transfers between devices: 13 us -> 0.01 us  [local(): lax.all_to_all(outgoing, 'loop', split_axis=0, concat_axis=0, tiled=True)]
  transfers between devices with their start and end apart: 2 -> 3, of which waited for: 1 -> 2; matrix products, arithmetic and copies ran while one was open for 74% -> 91% of each run, Pallas kernels for 0% -> 0%
where the time goes in v1:
time: 727 us; the launch traced here: 717 us
  local copies, waits for them, and re-layouts  529 us (73%)
  other arithmetic  91.7 us (13%)
  matrix products  46.9 us (6%)
  starting transfers between devices  22.1 us (3%)
  waiting for transfers between devices  16.5 us (2%)
  blocking collectives  9.39 us (1%)
    gather x16, local copies, waits for them, and re-layouts, turned_rows(): rotated = jnp.take(polar_rows, source_index, axis=2)  331 us
    reshape x8, local copies, waits for them, and re-layouts, turned_rows(): return rotated.reshape(block_rows * angle_count, radius_count * angle_count)  180 us
    select_n x16, other arithmetic, turned_rows(): rotated = jnp.take(polar_rows, source_index, axis=2)  85.3 us
    dot_general x8, matrix products, advance(): lax.dot_general(images, rotated, (((1,), (1,)), ((), ())), preferred_elem...  44 us
  transfers between devices with their start and end apart: 3, of which 2 were waited for; matrix products, arithmetic and copies ran while one was open for 91% of the time, Pallas kernels for 0%

profile of v1, /device:TPU:1, one launch (start us, length us, event | category | flops | bytes accessed | tf_op | source)
XLA Modules:
  0.0 717.4 jit_solution(16062217362010633349)
XLA Ops:
  3.3 12.0 %all-to-all-start.1 = ((bf16[64,2,3]{2,1,0:T(2,128)(2,1)}), bf16[64,2,3]{2,1,0:T(2,128)(2,1)S(1)}, u32[]{:S(2)}, u32[]{:S(2)}) async-start(bf16[64,2,3]{2,1,0:T(2,128)(2,1)} %bitcast.3), calls=%async_computation.1 | async-start | bytes 65536 | tf_op jit(solution)/shard_map/all_to_all | solution.py:95
  15.3 8.4 %all-to-all-done.1 = bf16[64,2,3]{2,1,0:T(2,128)(2,1)S(1)} async-done(((bf16[64,2,3]{2,1,0:T(2,128)(2,1)}), bf16[64,2,3]{2,1,0:T(2,128)(2,1)S(1)}, u32[]{:S(2)}, u32[]{:S(2)}) %all-to-all-start.1) | async-done | bytes 800 | tf_op jit(solution)/shard_map/all_to_all | solution.py:95
  25.8 4.7 all-to-all-start
  36.8 8.1 %all-to-all-done = bf16[64,2,3456]{2,1,0:T(2,128)(2,1)S(1)} async-done(((bf16[64,2,3456]{2,1,0:T(2,128)(2,1)}), bf16[64,2,3456]{2,1,0:T(2,128)(2,1)S(1)}, u32[]{:S(2)}, u32[]{:S(2)}) %all-to-all-start) | async-done | bytes 884768 | tf_op jit(solution)/shard_map/all_to_all | solution.py:65
  44.9 5.5 all-to-all-start.2
  50.8 648.6 %while.15 = (s32[]{:T(128)}, f32[128]{0:T(128)S(1)}, f32[128]{0:T(128)S(1)}, bf16[8,16,3456]{2,1,0:T(8,128)(2,1)S(1)}, bf16[128,3456]{1,0:T(8,128)(2,1)S(1)}, /*index=5*/s32[]{:T(128)}, s32[]{:T(128)}) while((s32[]{:T(128)}, f32[128]{0:T(128)S(1)}, f32[128]{0:T(128)S(1)}, bf16[8,16,3456]{2,1,0:T(8,128)(2,1)S(1)}, ...), condition=%wide.region_3.4_spmd.clone, body=%wide.region_0.3_spmd.clone.sunk | while | flops 1023913024 | bytes 74536928 | solution.py:54
  51.6 16.7 %gather_fusion = bf16[5184,16,48]{2,1,0:T(8,128)(2,1)} fusion(bf16[16,48,72]{1,0,2:T(8,128)(2,1)S(1)} %copy.31, s32[6144]{0:T(1024)S(1)} %pad_clamp_fusion.2), kind=kCustom, calls=%fused_computation.clone.clone.1 | custom fusion | bytes 15945984 | tf_op jit(solution)/shard_map/while/body/eval_jaxpr/jit(_take)/gather | solution.py:17
  68.4 24.6 %copy.32 = bf16[72,72,16,48]{1,3,0,2:T(8,128)(2,1)} copy(bf16[72,72,16,48]{3,2,1,0:T(8,128)(2,1)} %bitcast.36) | data formatting | bytes 15925248 | tf_op jit(solution)/shard_map/while/body/eval_jaxpr/jit(_take)/gather | solution.py:17
  93.0 10.6 %select_bitcast_fusion.2 = bf16[16,72,48,72]{3,2,1,0:T(8,128)(2,1)} fusion(bf16[72,72,16,48]{1,3,0,2:T(8,128)(2,1)} %copy.32, pred[72,72]{1,0:T(8,128)(4,1)S(1)} %compare_and_fusion.2), kind=kLoop, calls=%fused_computation.1.clone.1 | loop fusion | flops 3981312 | bytes 15930432 | tf_op jit(solution)/shard_map/while/body/eval_jaxpr/jit(_take)/select_n | solution.py:17
  103.7 22.5 %reshape.152 = bf16[1152,3456]{1,0:T(8,128)(2,1)} reshape(bf16[16,72,48,72]{3,2,1,0:T(8,128)(2,1)} %select_bitcast_fusion.2) | data formatting | bytes 15925248 | tf_op jit(solution)/shard_map/while/body/eval_jaxpr/reshape | solution.py:19
  126.2 5.5 fusion.45
  132.7 16.7 %gather_fusion = bf16[5184,16,48]{2,1,0:T(8,128)(2,1)} fusion(bf16[16,48,72]{1,0,2:T(8,128)(2,1)S(1)} %copy.31, s32[6144]{0:T(1024)S(1)} %pad_clamp_fusion.2), kind=kCustom, calls=%fused_computation.clone.clone.1 | custom fusion | bytes 15945984 | tf_op jit(solution)/shard_map/while/body/eval_jaxpr/jit(_take)/gather | solution.py:17
  149.4 24.6 %copy.32 = bf16[72,72,16,48]{1,3,0,2:T(8,128)(2,1)} copy(bf16[72,72,16,48]{3,2,1,0:T(8,128)(2,1)} %bitcast.36) | data formatting | bytes 15925248 | tf_op jit(solution)/shard_map/while/body/eval_jaxpr/jit(_take)/gather | solution.py:17
  174.1 10.6 %select_bitcast_fusion.2 = bf16[16,72,48,72]{3,2,1,0:T(8,128)(2,1)} fusion(bf16[72,72,16,48]{1,3,0,2:T(8,128)(2,1)} %copy.32, pred[72,72]{1,0:T(8,128)(4,1)S(1)} %compare_and_fusion.2), kind=kLoop, calls=%fused_computation.1.clone.1 | loop fusion | flops 3981312 | bytes 15930432 | tf_op jit(solution)/shard_map/while/body/eval_jaxpr/jit(_take)/select_n | solution.py:17
  184.7 22.5 %reshape.152 = bf16[1152,3456]{1,0:T(8,128)(2,1)} reshape(bf16[16,72,48,72]{3,2,1,0:T(8,128)(2,1)} %select_bitcast_fusion.2) | data formatting | bytes 15925248 | tf_op jit(solution)/shard_map/while/body/eval_jaxpr/reshape | solution.py:19
  207.2 5.5 fusion.45
  213.8 16.7 %gather_fusion = bf16[5184,16,48]{2,1,0:T(8,128)(2,1)} fusion(bf16[16,48,72]{1,0,2:T(8,128)(2,1)S(1)} %copy.31, s32[6144]{0:T(1024)S(1)} %pad_clamp_fusion.2), kind=kCustom, calls=%fused_computation.clone.clone.1 | custom fusion | bytes 15945984 | tf_op jit(solution)/shard_map/while/body/eval_jaxpr/jit(_take)/gather | solution.py:17
  230.5 24.6 %copy.32 = bf16[72,72,16,48]{1,3,0,2:T(8,128)(2,1)} copy(bf16[72,72,16,48]{3,2,1,0:T(8,128)(2,1)} %bitcast.36) | data formatting | bytes 15925248 | tf_op jit(solution)/shard_map/while/body/eval_jaxpr/jit(_take)/gather | solution.py:17
  255.2 10.6 %select_bitcast_fusion.2 = bf16[16,72,48,72]{3,2,1,0:T(8,128)(2,1)} fusion(bf16[72,72,16,48]{1,3,0,2:T(8,128)(2,1)} %copy.32, pred[72,72]{1,0:T(8,128)(4,1)S(1)} %compare_and_fusion.2), kind=kLoop, calls=%fused_computation.1.clone.1 | loop fusion | flops 3981312 | bytes 15930432 | tf_op jit(solution)/shard_map/while/body/eval_jaxpr/jit(_take)/select_n | solution.py:17
  265.8 22.5 %reshape.152 = bf16[1152,3456]{1,0:T(8,128)(2,1)} reshape(bf16[16,72,48,72]{3,2,1,0:T(8,128)(2,1)} %select_bitcast_fusion.2) | data formatting | bytes 15925248 | tf_op jit(solution)/shard_map/while/body/eval_jaxpr/reshape | solution.py:19
  288.3 5.5 fusion.45
  294.8 16.7 %gather_fusion = bf16[5184,16,48]{2,1,0:T(8,128)(2,1)} fusion(bf16[16,48,72]{1,0,2:T(8,128)(2,1)S(1)} %copy.31, s32[6144]{0:T(1024)S(1)} %pad_clamp_fusion.2), kind=kCustom, calls=%fused_computation.clone.clone.1 | custom fusion | bytes 15945984 | tf_op jit(solution)/shard_map/while/body/eval_jaxpr/jit(_take)/gather | solution.py:17
  311.6 24.6 %copy.32 = bf16[72,72,16,48]{1,3,0,2:T(8,128)(2,1)} copy(bf16[72,72,16,48]{3,2,1,0:T(8,128)(2,1)} %bitcast.36) | data formatting | bytes 15925248 | tf_op jit(solution)/shard_map/while/body/eval_jaxpr/jit(_take)/gather | solution.py:17
  336.2 10.6 %select_bitcast_fusion.2 = bf16[16,72,48,72]{3,2,1,0:T(8,128)(2,1)} fusion(bf16[72,72,16,48]{1,3,0,2:T(8,128)(2,1)} %copy.32, pred[72,72]{1,0:T(8,128)(4,1)S(1)} %compare_and_fusion.2), kind=kLoop, calls=%fused_computation.1.clone.1 | loop fusion | flops 3981312 | bytes 15930432 | tf_op jit(solution)/shard_map/while/body/eval_jaxpr/jit(_take)/select_n | solution.py:17
  346.9 22.5 %reshape.152 = bf16[1152,3456]{1,0:T(8,128)(2,1)} reshape(bf16[16,72,48,72]{3,2,1,0:T(8,128)(2,1)} %select_bitcast_fusion.2) | data formatting | bytes 15925248 | tf_op jit(solution)/shard_map/while/body/eval_jaxpr/reshape | solution.py:19
  369.4 5.5 fusion.45
  375.9 16.7 %gather_fusion = bf16[5184,16,48]{2,1,0:T(8,128)(2,1)} fusion(bf16[16,48,72]{1,0,2:T(8,128)(2,1)S(1)} %copy.31, s32[6144]{0:T(1024)S(1)} %pad_clamp_fusion.2), kind=kCustom, calls=%fused_computation.clone.clone.1 | custom fusion | bytes 15945984 | tf_op jit(solution)/shard_map/while/body/eval_jaxpr/jit(_take)/gather | solution.py:17
  392.6 24.6 %copy.32 = bf16[72,72,16,48]{1,3,0,2:T(8,128)(2,1)} copy(bf16[72,72,16,48]{3,2,1,0:T(8,128)(2,1)} %bitcast.36) | data formatting | bytes 15925248 | tf_op jit(solution)/shard_map/while/body/eval_jaxpr/jit(_take)/gather | solution.py:17
  417.3 10.6 %select_bitcast_fusion.2 = bf16[16,72,48,72]{3,2,1,0:T(8,128)(2,1)} fusion(bf16[72,72,16,48]{1,3,0,2:T(8,128)(2,1)} %copy.32, pred[72,72]{1,0:T(8,128)(4,1)S(1)} %compare_and_fusion.2), kind=kLoop, calls=%fused_computation.1.clone.1 | loop fusion | flops 3981312 | bytes 15930432 | tf_op jit(solution)/shard_map/while/body/eval_jaxpr/jit(_take)/select_n | solution.py:17
  427.9 22.5 %reshape.152 = bf16[1152,3456]{1,0:T(8,128)(2,1)} reshape(bf16[16,72,48,72]{3,2,1,0:T(8,128)(2,1)} %select_bitcast_fusion.2) | data formatting | bytes 15925248 | tf_op jit(solution)/shard_map/while/body/eval_jaxpr/reshape | solution.py:19
  450.4 5.5 fusion.45
  457.0 16.7 %gather_fusion = bf16[5184,16,48]{2,1,0:T(8,128)(2,1)} fusion(bf16[16,48,72]{1,0,2:T(8,128)(2,1)S(1)} %copy.31, s32[6144]{0:T(1024)S(1)} %pad_clamp_fusion.2), kind=kCustom, calls=%fused_computation.clone.clone.1 | custom fusion | bytes 15945984 | tf_op jit(solution)/shard_map/while/body/eval_jaxpr/jit(_take)/gather | solution.py:17
  473.7 24.6 %copy.32 = bf16[72,72,16,48]{1,3,0,2:T(8,128)(2,1)} copy(bf16[72,72,16,48]{3,2,1,0:T(8,128)(2,1)} %bitcast.36) | data formatting | bytes 15925248 | tf_op jit(solution)/shard_map/while/body/eval_jaxpr/jit(_take)/gather | solution.py:17
  498.4 10.6 %select_bitcast_fusion.2 = bf16[16,72,48,72]{3,2,1,0:T(8,128)(2,1)} fusion(bf16[72,72,16,48]{1,3,0,2:T(8,128)(2,1)} %copy.32, pred[72,72]{1,0:T(8,128)(4,1)S(1)} %compare_and_fusion.2), kind=kLoop, calls=%fused_computation.1.clone.1 | loop fusion | flops 3981312 | bytes 15930432 | tf_op jit(solution)/shard_map/while/body/eval_jaxpr/jit(_take)/select_n | solution.py:17
  509.0 22.5 %reshape.152 = bf16[1152,3456]{1,0:T(8,128)(2,1)} reshape(bf16[16,72,48,72]{3,2,1,0:T(8,128)(2,1)} %select_bitcast_fusion.2) | data formatting | bytes 15925248 | tf_op jit(solution)/shard_map/while/body/eval_jaxpr/reshape | solution.py:19
  531.5 5.5 fusion.45
  538.0 16.7 %gather_fusion = bf16[5184,16,48]{2,1,0:T(8,128)(2,1)} fusion(bf16[16,48,72]{1,0,2:T(8,128)(2,1)S(1)} %copy.31, s32[6144]{0:T(1024)S(1)} %pad_clamp_fusion.2), kind=kCustom, calls=%fused_computation.clone.clone.1 | custom fusion | bytes 15945984 | tf_op jit(solution)/shard_map/while/body/eval_jaxpr/jit(_take)/gather | solution.py:17
  554.8 24.6 %copy.32 = bf16[72,72,16,48]{1,3,0,2:T(8,128)(2,1)} copy(bf16[72,72,16,48]{3,2,1,0:T(8,128)(2,1)} %bitcast.36) | data formatting | bytes 15925248 | tf_op jit(solution)/shard_map/while/body/eval_jaxpr/jit(_take)/gather | solution.py:17
  579.4 10.6 %select_bitcast_fusion.2 = bf16[16,72,48,72]{3,2,1,0:T(8,128)(2,1)} fusion(bf16[72,72,16,48]{1,3,0,2:T(8,128)(2,1)} %copy.32, pred[72,72]{1,0:T(8,128)(4,1)S(1)} %compare_and_fusion.2), kind=kLoop, calls=%fused_computation.1.clone.1 | loop fusion | flops 3981312 | bytes 15930432 | tf_op jit(solution)/shard_map/while/body/eval_jaxpr/jit(_take)/select_n | solution.py:17
  590.1 22.5 %reshape.152 = bf16[1152,3456]{1,0:T(8,128)(2,1)} reshape(bf16[16,72,48,72]{3,2,1,0:T(8,128)(2,1)} %select_bitcast_fusion.2) | data formatting | bytes 15925248 | tf_op jit(solution)/shard_map/while/body/eval_jaxpr/reshape | solution.py:19
  612.6 5.5 fusion.45
  619.1 16.7 %gather_fusion = bf16[5184,16,48]{2,1,0:T(8,128)(2,1)} fusion(bf16[16,48,72]{1,0,2:T(8,128)(2,1)S(1)} %copy.31, s32[6144]{0:T(1024)S(1)} %pad_clamp_fusion.2), kind=kCustom, calls=%fused_computation.clone.clone.1 | custom fusion | bytes 15945984 | tf_op jit(solution)/shard_map/while/body/eval_jaxpr/jit(_take)/gather | solution.py:17
  635.9 24.6 %copy.32 = bf16[72,72,16,48]{1,3,0,2:T(8,128)(2,1)} copy(bf16[72,72,16,48]{3,2,1,0:T(8,128)(2,1)} %bitcast.36) | data formatting | bytes 15925248 | tf_op jit(solution)/shard_map/while/body/eval_jaxpr/jit(_take)/gather | solution.py:17
  660.5 10.6 %select_bitcast_fusion.2 = bf16[16,72,48,72]{3,2,1,0:T(8,128)(2,1)} fusion(bf16[72,72,16,48]{1,3,0,2:T(8,128)(2,1)} %copy.32, pred[72,72]{1,0:T(8,128)(4,1)S(1)} %compare_and_fusion.2), kind=kLoop, calls=%fused_computation.1.clone.1 | loop fusion | flops 3981312 | bytes 15930432 | tf_op jit(solution)/shard_map/while/body/eval_jaxpr/jit(_take)/select_n | solution.py:17
  671.2 22.5 %reshape.152 = bf16[1152,3456]{1,0:T(8,128)(2,1)} reshape(bf16[16,72,48,72]{3,2,1,0:T(8,128)(2,1)} %select_bitcast_fusion.2) | data formatting | bytes 15925248 | tf_op jit(solution)/shard_map/while/body/eval_jaxpr/reshape | solution.py:19
  693.6 5.5 fusion.45
  699.4 5.6 pmax.7
  705.0 4.8 reshape.123
  (133 shorter events, 26.2 us)
Async XLA Ops:
  0.6 50.1 %copy-start = (bf16[128,3456]{1,0:T(8,128)(2,1)S(1)}, bf16[128,3456]{1,0:T(8,128)(2,1)}, u32[]{:S(2)}) copy-start(bf16[128,3456]{1,0:T(8,128)(2,1)} %param.7) | copy-start | bytes 2654212
  3.3 20.4 %all-to-all-start.1 = ((bf16[64,2,3]{2,1,0:T(2,128)(2,1)}), bf16[64,2,3]{2,1,0:T(2,128)(2,1)S(1)}, u32[]{:S(2)}, u32[]{:S(2)}) async-start(bf16[64,2,3]{2,1,0:T(2,128)(2,1)} %bitcast.3), calls=%async_computation.1 | async-start | bytes 65536 | tf_op jit(solution)/shard_map/all_to_all | solution.py:95
  25.8 19.2 %all-to-all-start = ((bf16[64,2,3456]{2,1,0:T(2,128)(2,1)}), bf16[64,2,3456]{2,1,0:T(2,128)(2,1)S(1)}, u32[]{:S(2)}, u32[]{:S(2)}) async-start(bf16[64,2,3456]{2,1,0:T(2,128)(2,1)} %stack.14), calls=%async_computation | async-start | bytes 1769472 | tf_op jit(solution)/shard_map/all_to_all | solution.py:65
  35.4 15.4 %copy-start.5 = (bf16[128]{0:T(256)(128)(2,1)}, bf16[128]{0:T(256)(128)(2,1)S(1)}, u32[]{:S(2)}) copy-start(bf16[128]{0:T(256)(128)(2,1)S(1)} %slice_bitcast_fusion.1) | copy-start | bytes 772
  35.4 15.4 %copy-start.2 = (f32[128]{0:T(128)}, f32[128]{0:T(128)S(1)}, u32[]{:S(2)}) copy-start(f32[128]{0:T(128)S(1)} %get-tuple-element.104) | copy-start | bytes 1540
  44.9 660.1 %all-to-all-start.2 = ((bf16[64,2,3456]{2,1,0:T(2,128)(2,1)}), bf16[64,2,3456]{2,1,0:T(2,128)(2,1)}, u32[]{:S(2)}, u32[]{:S(2)}) async-start(bf16[64,2,3456]{2,1,0:T(2,128)(2,1)} %reshape.122), calls=%async_computation.2 | async-start | bytes 1769472 | tf_op jit(solution)/shard_map/all_to_all | solution.py:94
  50.8 659.1 %copy-start.1 = (f32[128,72]{1,0:T(8,128)S(1)}, f32[128,72]{1,0:T(8,128)}, u32[]{:S(2)}) copy-start(f32[128,72]{1,0:T(8,128)} %add_select_fusion.2) | copy-start | bytes 110596
  699.4 12.5 %copy-start.3 = (f32[128]{0:T(128)S(1)}, f32[128]{0:T(128)}, u32[]{:S(2)}) copy-start(f32[128]{0:T(128)} %copy-done.2) | copy-start | bytes 1540
  699.4 12.5 %copy-start.6 = (bf16[128]{0:T(256)(128)(2,1)S(1)}, bf16[128]{0:T(256)(128)(2,1)}, u32[]{:S(2)}) copy-start(bf16[128]{0:T(256)(128)(2,1)} %copy-done.5) | copy-start | bytes 772
  699.4 12.9 %copy-start.4 = (f32[4]{0:T(128)S(1)}, f32[4]{0:T(128)}, u32[]{:S(2)}) copy-start(f32[4]{0:T(128)} %convert_reduce_fusion) | copy-start | bytes 52
